TPU v7x, 256 devices: a whole 4x4x8 slice. The times are simulated.
256 devices in a mesh: dp: 4 (over x_lo, core), expert: 64 (over z, y, x_hi).
Axes of the slice: x: 4 (x_hi: 2, x_lo: 2; x = x_hi * 2 + x_lo), y: 4, z: 8, core: 2. Of those that a mesh axis runs over, the one named last changes fastest.
Arguments:
- prev_acts: bfloat16 [4, 64, 128, 3584], P('dp', 'expert'), may hold values from -6 to 6
- prev_cot: bfloat16 [4, 64, 128, 512], P('dp', 'expert'), may hold values from -0.59765625 to 0.59765625
- weights: bfloat16 [64, 3584, 512], P('expert', 'dp'), may hold values from -0.09375 to 0.09375
- first_moment: float32 [64, 3584, 512], P('expert', 'dp'), may hold values from -1.8 to 1.8
- second_moment: float32 [64, 3584, 512], P('expert', 'dp'), may hold values from 0.1 to 2
- tokens: bfloat16 [4, 64, 128, 3584], P('dp', 'expert'), may hold values from -6 to 6
- routing: int32 [4, 64, 128, 2], P('dp', 'expert'), may hold values from 0 to 15, all different within a row; in each aligned block of 128 rows (0 to 127, 128 to 255, ..., all dimensions but the last counted through in order) at most 24 rows name the same one
- gates: bfloat16 [4, 64, 128, 2], P('dp', 'expert'), may hold values from 0.19921875 to 1
- token_counts: int32 [4, 64], P('dp', 'expert'), may hold values from 64 to 128
- old_owner: int32 [16], replicated, may hold values from 0 to 15, each once
- new_owner: int32 [16], replicated, may hold values from 0 to 15, each once
Outputs:
- expert_hidden: bfloat16 [4, 64, 1536, 256], P('dp', 'expert')
- new_weights: bfloat16 [64, 3584, 512], P('expert', 'dp')
- new_first: float32 [64, 3584, 512], P('expert', 'dp')
- new_second: float32 [64, 3584, 512], P('expert', 'dp')
Inputs may be any that keep to these rules, and one draw needn't show every extreme that they name: `routing`: each token names 2 different hot experts; within the rows of one device no hot expert is named by more than 24 rows. `old_owner`: each is a permutation of the 16 groups. `new_owner`: each is a permutation of the 16 groups.
All inputs are finite; a program needn't handle non-finite values.
Results may differ from a plain program's by a relative error of at most 0.013.
Values may be sent and summed in bfloat16 or wider, within the bound.
No kernel may reach another device: no remote copies, remote signals or barrier semaphores. Data moves between devices by JAX's collectives and lax.ppermute only.
A program may use at most 128 MiB of HBM per device.

v0:
```python
import jax
import jax.numpy as jnp
from jax import lax
from jax.sharding import PartitionSpec as P

D = 3584
GRP = 4
beta_first = 0.9
beta_second = 0.95
learning = 0.00022
decay_rate = 0.1
epsilon = 1e-08
first_fix = 1.0 - 0.9**40
second_fix = 1.0 - 0.95**40


def adamw(weight_now, first_now, second_now, gradient):
    first_next = beta_first * first_now + (1.0 - beta_first) * gradient
    second_next = beta_second * second_now + (1.0 - beta_second) * gradient * gradient
    stepped = weight_now.astype(jnp.float32) * (1.0 - learning * decay_rate) - learning * (
        first_next / first_fix
    ) / (jnp.sqrt(second_next / second_fix) + epsilon)
    return (stepped.astype(jnp.bfloat16), jnp.stack([first_next, second_next]))


def migrate(weight_now, moment_stack, source, experts):
    rows_dev = weight_now.shape[0]
    width = weight_now.shape[1]
    layers = moment_stack.shape[0]
    piece_rows = rows_dev // experts
    weight_split = weight_now.reshape(experts, piece_rows, width)
    moment_split = moment_stack.reshape(layers, experts, piece_rows, width)
    weight_spread = lax.all_to_all(weight_split, "expert", split_axis=0, concat_axis=0, tiled=True)
    moment_spread = lax.all_to_all(moment_split, "expert", split_axis=1, concat_axis=1, tiled=True)
    weight_sorted = jnp.take(weight_spread, source, axis=0)
    moment_sorted = jnp.take(moment_spread, source, axis=1)
    weight_home = lax.all_to_all(weight_sorted, "expert", split_axis=0, concat_axis=0, tiled=True)
    moment_home = lax.all_to_all(moment_sorted, "expert", split_axis=1, concat_axis=1, tiled=True)
    return (weight_home.reshape(rows_dev, width), moment_home.reshape(layers, rows_dev, width))


def pack_tokens(token_block, route_block, gate_block, limit, hot_count, capacity):
    hot_index = jnp.arange(hot_count, dtype=jnp.int32)
    valid = jnp.arange(token_block.shape[0], dtype=jnp.int32) < limit
    hits = (route_block[:, :, None] == hot_index[None, None, :]) & valid[:, None, None]
    named = jnp.sum(hits.astype(jnp.int32), axis=1)
    scales = jnp.sum(jnp.where(hits, gate_block.astype(jnp.float32)[:, :, None], 0.0), axis=1)
    ranks = jnp.cumsum(named, axis=0) - named
    slots = jnp.arange(capacity, dtype=jnp.int32)
    placed = (ranks.T[:, None, :] == slots[None, :, None]) & (named.T[:, None, :] == 1)
    packed = jnp.einsum(
        "hct,td->hcd", placed.astype(jnp.bfloat16), token_block, preferred_element_type=jnp.float32
    ).astype(jnp.bfloat16)
    gate_scale = jnp.einsum("hct,th->hc", placed.astype(jnp.float32), scales).astype(jnp.bfloat16)
    return (packed, gate_scale)


def local(
    prev_acts,
    prev_cot,
    weights,
    first_moment,
    second_moment,
    tokens,
    routing,
    gates,
    token_counts,
    old_owner,
    new_owner,
):
    experts = lax.axis_size("expert")
    groups = experts // GRP
    token_slots = tokens.shape[2]
    capacity = min(token_slots, 3 * token_slots // groups)
    width = weights.shape[2]
    hidden_units = width // 2
    activations = prev_acts[0, 0]
    cotangent = prev_cot[0, 0]
    hot_index = jnp.arange(groups, dtype=jnp.int32)
    holder = jnp.sum(
        jnp.where(new_owner[None, :] == hot_index[:, None], hot_index[None, :], 0), axis=1
    )
    owners = jnp.arange(experts, dtype=jnp.int32)
    source = jnp.take(old_owner, jnp.take(holder, owners // GRP)) * GRP + owners % GRP
    columns = activations
    grads = lax.psum_scatter(
        lax.dot_general(
            columns, cotangent, (((0,), (0,)), ((), ())), preferred_element_type=jnp.float32
        ).astype(jnp.bfloat16),
        "dp",
        scatter_dimension=0,
        tiled=True,
    ).astype(jnp.float32)
    stepped, moment_stack = adamw(weights[0], first_moment[0], second_moment[0], grads)
    new_weight, moments = migrate(stepped, moment_stack, source, experts)
    packed, gate_scale = pack_tokens(
        tokens[0, 0], routing[0, 0], gates[0, 0], token_counts[0, 0], groups, capacity
    )
    to_group = jnp.take(packed, holder, axis=0)
    scale_group = jnp.take(gate_scale, holder, axis=0)
    scale_send = jnp.repeat(scale_group, GRP, axis=0)
    full_send = jnp.repeat(to_group, GRP, axis=0)
    received, scale_in = (
        lax.all_to_all(full_send, "expert", split_axis=0, concat_axis=0, tiled=True),
        lax.all_to_all(scale_send, "expert", split_axis=0, concat_axis=0, tiled=True),
    )
    token_rows = received.reshape(experts * capacity, D)
    columns = token_rows
    projected = jnp.dot(
        columns,
        lax.all_gather(new_weight, "dp", axis=0, tiled=True),
        preferred_element_type=jnp.float32,
    )
    scaling = scale_in.reshape(experts * capacity).astype(jnp.float32)
    result = (
        jax.nn.silu(projected[:, :hidden_units]) * projected[:, hidden_units:] * scaling[:, None]
    )
    hidden = result.astype(jnp.bfloat16).reshape(1, 1, experts * capacity, hidden_units)
    return (hidden, new_weight[None], moments[0][None], moments[1][None])


def solution(mesh):
    in_specs = (
        P("dp", "expert", None, None),
        P("dp", "expert", None, None),
        P("expert", "dp", None),
        P("expert", "dp", None),
        P("expert", "dp", None),
        P("dp", "expert", None, None),
        P("dp", "expert", None, None),
        P("dp", "expert", None, None),
        P("dp", "expert"),
        P(),
        P(),
    )
    out_specs = (
        P("dp", "expert", None, None),
        P("expert", "dp", None),
        P("expert", "dp", None),
        P("expert", "dp", None),
    )
    return jax.shard_map(local, mesh=mesh, in_specs=in_specs, out_specs=out_specs, check_vma=False)
```

profile of v0, /device:TPU:32, one launch (start us, length us, event | category | flops | bytes accessed | tf_op | source)
XLA Modules:
  0.0 610.4 jit_solution(13180646358381109086)
XLA Ops:
  8.4 3.8 convolution_convert_fusion
  13.4 45.2 %reduce-scatter.2.cloned.1.call-done = bf16[896,512]{1,0:T(8,128)(2,1)} async-done(((bf16[3584,512]{1,0:T(8,128)(2,1)}), bf16[896,512]{1,0:T(8,128)(2,1)}) %reduce-scatter.2.cloned.1.call-update) | async-done | bytes 917520 | tf_op jit(solution)/shard_map/reduce_scatter | solution.py:86
  58.6 5.4 fusion.2
  64.1 1.2 reshape.97
  65.3 12.7 %all-to-all-start.1 = ((bf16[64,14,512]{2,1,0:T(8,128)(2,1)}), bf16[64,14,512]{2,1,0:T(8,128)(2,1)S(1)}, u32[]{:S(2)}, u32[]{:S(2)}) async-start(bf16[64,14,512]{2,1,0:T(8,128)(2,1)} %reshape.97), calls=%async_computation.2 | async-start | bytes 2097152 | tf_op jit(solution)/shard_map/all_to_all | solution.py:33
  81.3 27.3 %all-to-all-done.1 = bf16[64,14,512]{2,1,0:T(8,128)(2,1)S(1)} async-done(((bf16[64,14,512]{2,1,0:T(8,128)(2,1)}), bf16[64,14,512]{2,1,0:T(8,128)(2,1)S(1)}, u32[]{:S(2)}, u32[]{:S(2)}) %all-to-all-start.1) | async-done | bytes 917536 | tf_op jit(solution)/shard_map/all_to_all | solution.py:33
  108.6 6.0 all-to-all-start.3
  116.3 9.2 %all-to-all-done.3 = bf16[64,1,24]{2,1,0:T(2,128)(2,1)S(1)} async-done(((bf16[64,1,24]{2,1,0:T(2,128)(2,1)}), bf16[64,1,24]{2,1,0:T(2,128)(2,1)S(1)}, u32[]{:S(2)}, u32[]{:S(2)}) %all-to-all-start.3) | async-done | bytes 3104 | tf_op jit(solution)/shard_map/all_to_all | solution.py:105
  125.5 5.6 all-to-all-start.2
  131.1 2.7 stack.10
  133.8 2.7 stack.9
  136.4 2.7 pad_maximum_fusion
  139.2 5.2 copy.44
  144.3 15.2 %all-to-all-done.2 = bf16[64,14,512]{2,1,0:T(8,128)(2,1)S(1)} async-done(((bf16[64,14,512]{2,1,0:T(8,128)(2,1)}), bf16[64,14,512]{2,1,0:T(8,128)(2,1)S(1)}, u32[]{:S(2)}, u32[]{:S(2)}) %all-to-all-start.2) | async-done | bytes 917536 | tf_op jit(solution)/shard_map/all_to_all | solution.py:37
  159.5 6.4 %all-to-all-start.4 = ((f32[2,64,14,512]{3,0,2,1:T(2,128)}), f32[2,64,14,512]{3,0,2,1:T(2,128)}, u32[]{:S(2)}, u32[]{:S(2)}) async-start(f32[2,64,14,512]{3,0,2,1:T(2,128)} %copy.44), calls=%async_computation.5 | async-start | bytes 7340032 | tf_op jit(solution)/shard_map/all_to_all | solution.py:34
  166.0 2.4 convolution_convert_fusion.1
  168.4 4.1 gather_fusion
  172.4 3.7 broadcast_select_fusion
  176.1 73.4 %all-to-all-done.4 = f32[2,64,14,512]{3,0,2,1:T(2,128)} async-done(((f32[2,64,14,512]{3,0,2,1:T(2,128)}), f32[2,64,14,512]{3,0,2,1:T(2,128)}, u32[]{:S(2)}, u32[]{:S(2)}) %all-to-all-start.4) | async-done | bytes 3670048 | tf_op jit(solution)/shard_map/all_to_all | solution.py:34
  249.5 6.6 %broadcast_in_dim.92 = bf16[16,4,24,3584]{3,2,1,0:T(8,128)(2,1)} broadcast(bf16[16,24,3584]{2,1,0:T(8,128)(2,1)} %broadcast_select_fusion), dimensions={0,2,3} | broadcast | bytes 13762560 | tf_op jit(solution)/shard_map/broadcast_in_dim | solution.py:102
  256.1 7.1 %all-to-all-start = ((bf16[64,24,3584]{2,1,0:T(8,128)(2,1)}), bf16[64,24,3584]{2,1,0:T(8,128)(2,1)}, u32[]{:S(2)}, u32[]{:S(2)}) async-start(bf16[64,24,3584]{2,1,0:T(8,128)(2,1)} %bitcast.52), calls=%async_computation | async-start | bytes 22020096 | tf_op jit(solution)/shard_map/all_to_all | solution.py:104
  263.2 1.2 reshape.98
  264.4 8.1 %gather_fusion.3 = f32[64,2,14,512]{3,1,2,0:T(2,128)} fusion(f32[2,64,14,512]{3,0,2,1:T(2,128)} %all-to-all-done.4, s32[1024]{0:T(1024)S(1)} %pad_clamp_fusion), kind=kCustom, calls=%fused_computation.5 | custom fusion | bytes 7340288 | tf_op jit(solution)/shard_map/jit(_take)/gather | solution.py:36
  272.5 5.8 select_bitcast_fusion
  278.3 224.6 %all-to-all-done = bf16[64,24,3584]{2,1,0:T(8,128)(2,1)} async-done(((bf16[64,24,3584]{2,1,0:T(8,128)(2,1)}), bf16[64,24,3584]{2,1,0:T(8,128)(2,1)}, u32[]{:S(2)}, u32[]{:S(2)}) %all-to-all-start) | async-done | bytes 11010080 | tf_op jit(solution)/shard_map/all_to_all | solution.py:104
  502.9 9.1 %all-to-all-start.5 = ((f32[2,64,14,512]{3,0,2,1:T(2,128)}), f32[2,64,14,512]{3,0,2,1:T(2,128)}, u32[]{:S(2)}, u32[]{:S(2)}) async-start(f32[2,64,14,512]{3,0,2,1:T(2,128)} %select_bitcast_fusion), calls=%async_computation.6 | async-start | bytes 7340032 | tf_op jit(solution)/shard_map/all_to_all | solution.py:38
  513.4 9.7 %fusion.23 = f32[1536,512]{1,0:T(8,128)S(1)} fusion(bf16[1536,3584]{1,0:T(8,128)(2,1)} %bitcast.9, bf16[3584,512]{1,0:T(8,128)(2,1)} %all-gather.2.cloned.1.call-done), kind=kOutput, calls=%fused_computation.65 | convolution fusion | flops 5637144576 | bytes 17825792 | tf_op jit(solution)/shard_map/dot_general | solution.py:109
  523.1 1.3 fusion.7
  524.4 69.9 %all-to-all-done.5 = f32[2,64,14,512]{3,0,2,1:T(2,128)} async-done(((f32[2,64,14,512]{3,0,2,1:T(2,128)}), f32[2,64,14,512]{3,0,2,1:T(2,128)}, u32[]{:S(2)}, u32[]{:S(2)}) %all-to-all-start.5) | async-done | bytes 3670048 | tf_op jit(solution)/shard_map/all_to_all | solution.py:38
  594.3 6.4 %fusion.22 = (f32[1,64,14,512]{3,0,2,1:T(1,128)S(1)}, f32[1,64,14,512]{3,0,2,1:T(1,128)S(1)}) fusion(f32[2,64,14,512]{3,0,2,1:T(2,128)} %all-to-all-done.5), kind=kLoop, calls=%fused_computation.64 | loop fusion | bytes 7340032 | tf_op jit(solution)/shard_map/slice | solution.py:119
  600.7 1.4 copy.45
  602.1 1.4 copy.46
  (53 shorter events, 8.1 us)
Async XLA Ops:
  7.2 1.2 copy-start
  7.2 51.4 %reduce-scatter.2.cloned.1.call-start = ((), (), s32[]{:S(2)}) async-start(), calls=%async_computation.7 | async-start | bytes 4587520 | tf_op jit(solution)/shard_map/reduce_scatter | solution.py:86
  12.2 0.8 copy-start.5
  12.2 1.2 copy-start.6
  12.2 46.4 %copy-start.3 = (f32[1,896,512]{2,1,0:T(8,128)S(1)}, f32[1,896,512]{2,1,0:T(8,128)}, u32[]{:S(2)}) copy-start(f32[1,896,512]{2,1,0:T(8,128)} %param.16) | copy-start | bytes 5505028
  64.1 14.1 %copy-start.7 = (s32[16]{0:T(128)S(1)}, s32[16]{0:T(128)}, u32[]{:S(2)}) copy-start(s32[16]{0:T(128)} %param.23) | copy-start | bytes 196
  65.3 15.2 %copy-start.2 = (s32[16]{0:T(128)S(1)}, s32[16]{0:T(128)}, u32[]{:S(2)}) copy-start(s32[16]{0:T(128)} %param.22) | copy-start | bytes 196
  65.3 43.3 %all-to-all-start.1 = ((bf16[64,14,512]{2,1,0:T(8,128)(2,1)}), bf16[64,14,512]{2,1,0:T(8,128)(2,1)S(1)}, u32[]{:S(2)}, u32[]{:S(2)}) async-start(bf16[64,14,512]{2,1,0:T(8,128)(2,1)} %reshape.97), calls=%async_computation.2 | async-start | bytes 2097152 | tf_op jit(solution)/shard_map/all_to_all | solution.py:33
  108.6 16.9 %all-to-all-start.3 = ((bf16[64,1,24]{2,1,0:T(2,128)(2,1)}), bf16[64,1,24]{2,1,0:T(2,128)(2,1)S(1)}, u32[]{:S(2)}, u32[]{:S(2)}) async-start(bf16[64,1,24]{2,1,0:T(2,128)(2,1)} %copy.43), calls=%async_computation.4 | async-start | bytes 65536 | tf_op jit(solution)/shard_map/all_to_all | solution.py:105
  125.5 34.0 %all-to-all-start.2 = ((bf16[64,14,512]{2,1,0:T(8,128)(2,1)}), bf16[64,14,512]{2,1,0:T(8,128)(2,1)S(1)}, u32[]{:S(2)}, u32[]{:S(2)}) async-start(bf16[64,14,512]{2,1,0:T(8,128)(2,1)} %broadcast_select_fusion.1), calls=%async_computation.3 | async-start | bytes 2097152 | tf_op jit(solution)/shard_map/all_to_all | solution.py:37
  144.3 21.6 %copy-start.4 = (bf16[1,1,128,3584]{3,2,1,0:T(8,128)(2,1)S(1)}, bf16[1,1,128,3584]{3,2,1,0:T(8,128)(2,1)}, u32[]{:S(2)}) copy-start(bf16[1,1,128,3584]{3,2,1,0:T(8,128)(2,1)} %param.18) | copy-start | bytes 2752516
  159.5 90.0 %all-to-all-start.4 = ((f32[2,64,14,512]{3,0,2,1:T(2,128)}), f32[2,64,14,512]{3,0,2,1:T(2,128)}, u32[]{:S(2)}, u32[]{:S(2)}) async-start(f32[2,64,14,512]{3,0,2,1:T(2,128)} %copy.44), calls=%async_computation.5 | async-start | bytes 7340032 | tf_op jit(solution)/shard_map/all_to_all | solution.py:34
  256.1 246.9 %all-to-all-start = ((bf16[64,24,3584]{2,1,0:T(8,128)(2,1)}), bf16[64,24,3584]{2,1,0:T(8,128)(2,1)}, u32[]{:S(2)}, u32[]{:S(2)}) async-start(bf16[64,24,3584]{2,1,0:T(8,128)(2,1)} %bitcast.52), calls=%async_computation | async-start | bytes 22020096 | tf_op jit(solution)/shard_map/all_to_all | solution.py:104
  263.2 250.2 %all-gather.2.cloned.1.call-start = ((), (), s32[]{:S(2)}) async-start(), calls=%async_computation.8 | async-start | bytes 4587520 | tf_op jit(solution)/shard_map/all_gather | solution.py:111
  502.9 91.4 %all-to-all-start.5 = ((f32[2,64,14,512]{3,0,2,1:T(2,128)}), f32[2,64,14,512]{3,0,2,1:T(2,128)}, u32[]{:S(2)}, u32[]{:S(2)}) async-start(f32[2,64,14,512]{3,0,2,1:T(2,128)} %select_bitcast_fusion), calls=%async_computation.6 | async-start | bytes 7340032 | tf_op jit(solution)/shard_map/all_to_all | solution.py:38
  602.1 1.5 copy-start.1
Sparse Core Ops, SparseCore 0:
  12.3 46.2 reduce-scatter.1
  266.4 78.0 all-gather.1
where the time goes:
time: 611 us; the launch traced here: 610 us
  waiting for transfers between devices  465 us (76%)
  starting transfers between devices  47 us (8%)
  local copies, waits for them, and re-layouts  46.9 us (8%)
  other arithmetic  20.7 us (3%)
  matrix products  16.1 us (3%)
  between operations  15 us (2%)
    all_to_all x1, waiting for transfers between devices, local(): lax.all_to_all(full_send, 'expert', split_axis=0, concat_axis=0, tiled=True)  225 us
    all_to_all x1, waiting for transfers between devices, migrate(): lax.all_to_all(moment_split, 'expert', split_axis=1, concat_axis=1, tiled...  73.4 us
    all_to_all x1, waiting for transfers between devices, migrate(): lax.all_to_all(moment_sorted, 'expert', split_axis=1, concat_axis=1, tile...  69.9 us
    reduce_scatter x1, waiting for transfers between devices, local(): lax.psum_scatter(lax.dot_general(columns, cotangent, (((0,), (0,)), ((),...  45.2 us
    all_to_all x1, waiting for transfers between devices, migrate(): lax.all_to_all(weight_split, 'expert', split_axis=0, concat_axis=0, tiled...  27.3 us
    all_to_all x1, waiting for transfers between devices, migrate(): lax.all_to_all(weight_sorted, 'expert', split_axis=0, concat_axis=0, tile...  15.2 us
    all_to_all x1, starting transfers between devices, migrate(): lax.all_to_all(weight_split, 'expert', split_axis=0, concat_axis=0, tiled...  12.7 us
  transfers between devices with their start and end apart: 8, of which 7 were waited for; matrix products, arithmetic and copies ran while one was open for 9% of the time, Pallas kernels for 0%

commit v1 on v0

--- a/solution.py
+++ b/solution.py
@@ -2,6 +2,7 @@
 import jax.numpy as jnp
 from jax import lax
 from jax.sharding import PartitionSpec as P
+from jax.lax import all_to_all, axis_size
 
 D = 3584
 GRP = 4
@@ -35,7 +36,12 @@
     weight_sorted = jnp.take(weight_spread, source, axis=0)
     moment_sorted = jnp.take(moment_spread, source, axis=1)
     weight_home = lax.all_to_all(weight_sorted, "expert", split_axis=0, concat_axis=0, tiled=True)
-    moment_home = lax.all_to_all(moment_sorted, "expert", split_axis=1, concat_axis=1, tiled=True)
+    moment_home = jnp.concatenate(
+        all_to_all(
+            jnp.stack(jnp.split(moment_sorted, axis_size("expert"), axis=1)), "expert", 0, 0
+        ),
+        axis=1,
+    )
     return (weight_home.reshape(rows_dev, width), moment_home.reshape(layers, rows_dev, width))
 
 

time: 611 us -> 611 us (level)
  local copies, waits for them, and re-layouts: 46.9 us -> 86.6 us
  waiting for transfers between devices: 465 us -> 427 us
    unnamed x18 -> x81, local copies, waits for them, and re-layouts: 3.99 us -> 43.1 us
    all_to_all x1, waiting for transfers between devices: 225 us -> 187 us  [local(): lax.all_to_all(full_send, 'expert', split_axis=0, concat_axis=0, tiled=True)]
  transfers between devices with their start and end apart: 8 -> 8, of which waited for: 7 -> 7; matrix products, arithmetic and copies ran while one was open for 9% -> 15% of each run, Pallas kernels for 0% -> 0%
where the time goes in v1:
time: 611 us; the launch traced here: 610 us
  waiting for transfers between devices  427 us (70%)
  local copies, waits for them, and re-layouts  86.6 us (14%)
  starting transfers between devices  46.9 us (8%)
  other arithmetic  19.1 us (3%)
  matrix products  16.1 us (3%)
  between operations  15 us (2%)
    all_to_all x1, waiting for transfers between devices, local(): lax.all_to_all(full_send, 'expert', split_axis=0, concat_axis=0, tiled=True)  187 us
    all_to_all x1, waiting for transfers between devices, migrate(): lax.all_to_all(moment_split, 'expert', split_axis=1, concat_axis=1, tiled...  73.5 us
    all_to_all x1, waiting for transfers between devices, migrate(): all_to_all(jnp.stack(jnp.split(moment_sorted, axis_size('expert'), axis=1...  69.9 us
    reduce_scatter x1, waiting for transfers between devices, local(): lax.psum_scatter(lax.dot_general(columns, cotangent, (((0,), (0,)), ((),...  45.2 us
    unnamed x81, local copies, waits for them, and re-layouts  43.1 us
    all_to_all x1, waiting for transfers between devices, migrate(): lax.all_to_all(weight_split, 'expert', split_axis=0, concat_axis=0, tiled...  27.3 us
    all_to_all x1, waiting for transfers between devices, migrate(): lax.all_to_all(weight_sorted, 'expert', split_axis=0, concat_axis=0, tile...  15.2 us
    all_to_all x1, starting transfers between devices, migrate(): lax.all_to_all(weight_split, 'expert', split_axis=0, concat_axis=0, tiled...  12.6 us
  transfers between devices with their start and end apart: 8, of which 7 were waited for; matrix products, arithmetic and copies ran while one was open for 15% of the time, Pallas kernels for 0%

profile of v1, /device:TPU:32, one launch (start us, length us, event | category | flops | bytes accessed | tf_op | source)
XLA Modules:
  0.0 610.4 jit_solution(9138491471409374206)
XLA Ops:
  8.4 3.8 convolution_convert_fusion
  13.4 45.2 %reduce-scatter.2.cloned.1.call-done = bf16[896,512]{1,0:T(8,128)(2,1)} async-done(((bf16[3584,512]{1,0:T(8,128)(2,1)}), bf16[896,512]{1,0:T(8,128)(2,1)}) %reduce-scatter.2.cloned.1.call-update) | async-done | bytes 917520 | tf_op jit(solution)/shard_map/reduce_scatter | solution.py:92
  58.6 5.7 fusion.2
  64.3 1.2 reshape.99
  65.5 12.6 %all-to-all-start.1 = ((bf16[64,14,512]{2,1,0:T(8,128)(2,1)}), bf16[64,14,512]{2,1,0:T(8,128)(2,1)S(1)}, u32[]{:S(2)}, u32[]{:S(2)}) async-start(bf16[64,14,512]{2,1,0:T(8,128)(2,1)} %reshape.99), calls=%async_computation.2 | async-start | bytes 2097152 | tf_op jit(solution)/shard_map/all_to_all | solution.py:34
  81.4 27.3 %all-to-all-done.1 = bf16[64,14,512]{2,1,0:T(8,128)(2,1)S(1)} async-done(((bf16[64,14,512]{2,1,0:T(8,128)(2,1)}), bf16[64,14,512]{2,1,0:T(8,128)(2,1)S(1)}, u32[]{:S(2)}, u32[]{:S(2)}) %all-to-all-start.1) | async-done | bytes 917536 | tf_op jit(solution)/shard_map/all_to_all | solution.py:34
  108.7 6.0 all-to-all-start.3
  116.4 9.2 %all-to-all-done.3 = bf16[64,1,24]{2,1,0:T(2,128)(2,1)S(1)} async-done(((bf16[64,1,24]{2,1,0:T(2,128)(2,1)}), bf16[64,1,24]{2,1,0:T(2,128)(2,1)S(1)}, u32[]{:S(2)}, u32[]{:S(2)}) %all-to-all-start.3) | async-done | bytes 3104 | tf_op jit(solution)/shard_map/all_to_all | solution.py:111
  125.6 5.6 all-to-all-start.2
  131.2 2.7 stack.205
  133.9 2.7 stack.204
  136.5 2.7 pad_maximum_fusion
  139.3 5.1 copy.44
  144.4 15.2 %all-to-all-done.2 = bf16[64,14,512]{2,1,0:T(8,128)(2,1)S(1)} async-done(((bf16[64,14,512]{2,1,0:T(8,128)(2,1)}), bf16[64,14,512]{2,1,0:T(8,128)(2,1)S(1)}, u32[]{:S(2)}, u32[]{:S(2)}) %all-to-all-start.2) | async-done | bytes 917536 | tf_op jit(solution)/shard_map/all_to_all | solution.py:38
  159.6 6.4 %all-to-all-start.4 = ((f32[2,64,14,512]{3,0,2,1:T(2,128)}), f32[2,64,14,512]{3,0,2,1:T(2,128)}, u32[]{:S(2)}, u32[]{:S(2)}) async-start(f32[2,64,14,512]{3,0,2,1:T(2,128)} %copy.44), calls=%async_computation.5 | async-start | bytes 7340032 | tf_op jit(solution)/shard_map/all_to_all | solution.py:35
  166.1 2.4 convolution_convert_fusion.1
  168.5 4.0 gather_fusion
  172.5 3.6 broadcast_select_fusion
  176.1 73.5 %all-to-all-done.4 = f32[2,64,14,512]{3,0,2,1:T(2,128)} async-done(((f32[2,64,14,512]{3,0,2,1:T(2,128)}), f32[2,64,14,512]{3,0,2,1:T(2,128)}, u32[]{:S(2)}, u32[]{:S(2)}) %all-to-all-start.4) | async-done | bytes 3670048 | tf_op jit(solution)/shard_map/all_to_all | solution.py:35
  249.6 6.6 %broadcast_in_dim.92 = bf16[16,4,24,3584]{3,2,1,0:T(8,128)(2,1)} broadcast(bf16[16,24,3584]{2,1,0:T(8,128)(2,1)} %broadcast_select_fusion), dimensions={0,2,3} | broadcast | bytes 13762560 | tf_op jit(solution)/shard_map/broadcast_in_dim | solution.py:108
  256.2 7.1 %all-to-all-start = ((bf16[64,24,3584]{2,1,0:T(8,128)(2,1)}), bf16[64,24,3584]{2,1,0:T(8,128)(2,1)}, u32[]{:S(2)}, u32[]{:S(2)}) async-start(bf16[64,24,3584]{2,1,0:T(8,128)(2,1)} %bitcast.309), calls=%async_computation | async-start | bytes 22020096 | tf_op jit(solution)/shard_map/all_to_all | solution.py:110
  263.3 1.2 reshape.100
  264.6 8.1 %gather_fusion.3 = f32[64,2,14,512]{3,1,2,0:T(2,128)} fusion(f32[2,64,14,512]{3,0,2,1:T(2,128)} %all-to-all-done.4, s32[1024]{0:T(1024)S(1)} %pad_clamp_fusion), kind=kCustom, calls=%fused_computation.5 | custom fusion | bytes 7340288 | tf_op jit(solution)/shard_map/jit(_take)/gather | solution.py:37
  272.6 4.0 select_bitcast_fusion
  316.5 186.6 %all-to-all-done = bf16[64,24,3584]{2,1,0:T(8,128)(2,1)} async-done(((bf16[64,24,3584]{2,1,0:T(8,128)(2,1)}), bf16[64,24,3584]{2,1,0:T(8,128)(2,1)}, u32[]{:S(2)}, u32[]{:S(2)}) %all-to-all-start) | async-done | bytes 11010080 | tf_op jit(solution)/shard_map/all_to_all | solution.py:110
  503.1 9.1 %all-to-all-start.5 = ((f32[64,2,1,14,512]{4,1,3,2,0:T(2,128)}), f32[64,2,1,14,512]{4,1,3,2,0:T(2,128)}, u32[]{:S(2)}, u32[]{:S(2)}) async-start(f32[64,2,1,14,512]{4,1,3,2,0:T(2,128)} %constant_dynamic-update-slice_fusion), calls=%async_computation.6 | async-start | bytes 7340032 | tf_op jit(solution)/shard_map/all_to_all | solution.py:40
  513.5 9.7 %fusion.23 = f32[1536,512]{1,0:T(8,128)S(1)} fusion(bf16[1536,3584]{1,0:T(8,128)(2,1)} %bitcast.9, bf16[3584,512]{1,0:T(8,128)(2,1)} %all-gather.2.cloned.1.call-done), kind=kOutput, calls=%fused_computation.193 | convolution fusion | flops 5637144576 | bytes 17825792 | tf_op jit(solution)/shard_map/dot_general | solution.py:115
  523.2 1.3 fusion.7
  524.6 69.9 %all-to-all-done.5 = f32[64,2,1,14,512]{4,1,3,2,0:T(2,128)} async-done(((f32[64,2,1,14,512]{4,1,3,2,0:T(2,128)}), f32[64,2,1,14,512]{4,1,3,2,0:T(2,128)}, u32[]{:S(2)}, u32[]{:S(2)}) %all-to-all-start.5) | async-done | bytes 3670048 | tf_op jit(solution)/shard_map/all_to_all | solution.py:40
  594.4 6.4 %fusion.22 = (f32[1,64,1,14,512]{4,0,3,2,1:T(1,128)S(1)}, f32[1,64,1,14,512]{4,0,3,2,1:T(1,128)S(1)}) fusion(f32[2,64,1,14,512]{4,0,3,2,1:T(2,128)} %bitcast.87), kind=kLoop, calls=%fused_computation.192 | loop fusion | bytes 7340032 | tf_op jit(solution)/shard_map/slice | solution.py:125
  600.8 1.4 copy.45
  602.2 1.4 copy.46
  (116 shorter events, 47.8 us)
Async XLA Ops:
  7.2 1.2 copy-start
  7.2 51.4 %reduce-scatter.2.cloned.1.call-start = ((), (), s32[]{:S(2)}) async-start(), calls=%async_computation.7 | async-start | bytes 4587520 | tf_op jit(solution)/shard_map/reduce_scatter | solution.py:92
  12.2 0.8 copy-start.5
  12.2 1.1 copy-start.6
  12.2 46.4 %copy-start.3 = (bf16[1,896,512]{2,1,0:T(8,128)(2,1)S(1)}, bf16[1,896,512]{2,1,0:T(8,128)(2,1)}, u32[]{:S(2)}) copy-start(bf16[1,896,512]{2,1,0:T(8,128)(2,1)} %param.15) | copy-start | bytes 2752516
  64.3 14.0 %copy-start.7 = (s32[16]{0:T(128)S(1)}, s32[16]{0:T(128)}, u32[]{:S(2)}) copy-start(s32[16]{0:T(128)} %param.23) | copy-start | bytes 196
  64.3 16.3 %copy-start.2 = (s32[16]{0:T(128)S(1)}, s32[16]{0:T(128)}, u32[]{:S(2)}) copy-start(s32[16]{0:T(128)} %param.22) | copy-start | bytes 196
  65.5 43.1 %all-to-all-start.1 = ((bf16[64,14,512]{2,1,0:T(8,128)(2,1)}), bf16[64,14,512]{2,1,0:T(8,128)(2,1)S(1)}, u32[]{:S(2)}, u32[]{:S(2)}) async-start(bf16[64,14,512]{2,1,0:T(8,128)(2,1)} %reshape.99), calls=%async_computation.2 | async-start | bytes 2097152 | tf_op jit(solution)/shard_map/all_to_all | solution.py:34
  108.7 16.9 %all-to-all-start.3 = ((bf16[64,1,24]{2,1,0:T(2,128)(2,1)}), bf16[64,1,24]{2,1,0:T(2,128)(2,1)S(1)}, u32[]{:S(2)}, u32[]{:S(2)}) async-start(bf16[64,1,24]{2,1,0:T(2,128)(2,1)} %copy.43), calls=%async_computation.4 | async-start | bytes 65536 | tf_op jit(solution)/shard_map/all_to_all | solution.py:111
  125.6 34.0 %all-to-all-start.2 = ((bf16[64,14,512]{2,1,0:T(8,128)(2,1)}), bf16[64,14,512]{2,1,0:T(8,128)(2,1)S(1)}, u32[]{:S(2)}, u32[]{:S(2)}) async-start(bf16[64,14,512]{2,1,0:T(8,128)(2,1)} %broadcast_select_fusion.1), calls=%async_computation.3 | async-start | bytes 2097152 | tf_op jit(solution)/shard_map/all_to_all | solution.py:38
  144.4 21.7 %copy-start.4 = (bf16[1,1,128,3584]{3,2,1,0:T(8,128)(2,1)S(1)}, bf16[1,1,128,3584]{3,2,1,0:T(8,128)(2,1)}, u32[]{:S(2)}) copy-start(bf16[1,1,128,3584]{3,2,1,0:T(8,128)(2,1)} %param.18) | copy-start | bytes 2752516
  159.6 90.0 %all-to-all-start.4 = ((f32[2,64,14,512]{3,0,2,1:T(2,128)}), f32[2,64,14,512]{3,0,2,1:T(2,128)}, u32[]{:S(2)}, u32[]{:S(2)}) async-start(f32[2,64,14,512]{3,0,2,1:T(2,128)} %copy.44), calls=%async_computation.5 | async-start | bytes 7340032 | tf_op jit(solution)/shard_map/all_to_all | solution.py:35
  256.2 246.9 %all-to-all-start = ((bf16[64,24,3584]{2,1,0:T(8,128)(2,1)}), bf16[64,24,3584]{2,1,0:T(8,128)(2,1)}, u32[]{:S(2)}, u32[]{:S(2)}) async-start(bf16[64,24,3584]{2,1,0:T(8,128)(2,1)} %bitcast.309), calls=%async_computation | async-start | bytes 22020096 | tf_op jit(solution)/shard_map/all_to_all | solution.py:110
  263.3 250.2 %all-gather.2.cloned.1.call-start = ((), (), s32[]{:S(2)}) async-start(), calls=%async_computation.8 | async-start | bytes 4587520 | tf_op jit(solution)/shard_map/all_gather | solution.py:117
  503.1 91.4 %all-to-all-start.5 = ((f32[64,2,1,14,512]{4,1,3,2,0:T(2,128)}), f32[64,2,1,14,512]{4,1,3,2,0:T(2,128)}, u32[]{:S(2)}, u32[]{:S(2)}) async-start(f32[64,2,1,14,512]{4,1,3,2,0:T(2,128)} %constant_dynamic-update-slice_fusion), calls=%async_computation.6 | async-start | bytes 7340032 | tf_op jit(solution)/shard_map/all_to_all | solution.py:40
  600.8 2.8 copy-start.1
Sparse Core Ops, SparseCore 0:
  12.3 46.2 reduce-scatter.1
  266.5 78.0 all-gather.1
